TPU v7x, 256 devices: a whole 4x4x8 slice. The times are simulated.
256 devices in a mesh: gx: 8 (over y, core), gy: 32 (over z, x).
Axes of the slice: x: 4, y: 4, z: 8, core: 2. Of those that a mesh axis runs over, the one named last changes fastest.
Arguments:
- source_field: float32 [4096, 64, 256], P('gx', 'gy'), may hold values from -6 to 6
- permeability: float32 [4096, 64, 256], P('gx', 'gy'), may hold values from 0.3 to 3
- layer_ids: int32 [256], replicated, may hold values from 0 to 3, as said below
- inverse_fine: float32 [4, 4096, 512], P(None, 'gx'), as said below
- couple_fine: float32 [2, 4, 8], P(None, None, 'gx'), may hold values from 0.35 to 0.7
- inverse_coarse: float32 [4, 4096, 512], P(None, 'gx'), as said below
- couple_coarse: float32 [2, 4, 8], P(None, None, 'gx'), may hold values from 0.35 to 0.7
- owner_map: int32 [32, 1], replicated, may hold values from 0 to 7
Outputs:
- solution_fine: float32 [4096, 64, 256], P('gx', 'gy')
- residual_fine: float32 [4096, 64, 256], P('gx', 'gy')
- solution_coarse: float32 [4096, 32, 256], P('gx', 'gy')
Inputs may be any that keep to these rules, and one draw needn't show every extreme that they name: owner_map names the aggregate of each level-6 plane; every aggregate below 8 holds at least one plane. `layer_ids`: every rock type names the same number of z cells. `inverse_fine`: each block is a positive-definite dense matrix with a diagonal dominating each line solve's coupling. `inverse_coarse`: each block is a positive-definite dense matrix with a diagonal dominating each line solve's coupling.
All inputs are finite; a program needn't handle non-finite values.
Results may differ from a plain program's by a relative error of at most 0.00012.
Values sent between devices are 32-bit elements; how exact they have to be, the bound alone decides.
No kernel may reach another device: no remote copies, remote signals or barrier semaphores. Data moves between devices by JAX's collectives and lax.ppermute only.
A program may use at most 128 MiB of HBM per device.

v0:
```python
import jax
import jax.numpy as jnp
from jax import lax
from jax.sharding import PartitionSpec as P

NSWEEP = 3
PRECISE = lax.Precision.HIGHEST
WEIGHTS = (0.5, 0.5, 0.15, 0.15, 0.05, 0.05)
STORAGE = 0.1


def with_halo(array, sides, width):
    for axis, dim in sides:
        peers, length = (lax.axis_size(axis), array.shape[dim])
        up = [(i, (i + 1) % peers) for i in range(peers - 1)]
        down = [(j, i) for i, j in up]
        last = lax.slice_in_dim(array, length - width, length, axis=dim)
        leading = lax.slice_in_dim(array, 0, width, axis=dim)
        before = lax.ppermute(last, axis, up)
        after = lax.ppermute(leading, axis, down)
        array = jnp.concatenate([before, array, after], axis=dim)
    return array


def neighbours(padded):
    return [
        padded[:-2, 1:-1, 1:-1],
        padded[2:, 1:-1, 1:-1],
        padded[1:-1, :-2, 1:-1],
        padded[1:-1, 2:, 1:-1],
        padded[1:-1, 1:-1, :-2],
        padded[1:-1, 1:-1, 2:],
    ]


def face_terms(padded):
    centre = padded[1:-1, 1:-1, 1:-1]
    return [
        weight * 2.0 * centre * beside / (centre + beside)
        for weight, beside in zip(WEIGHTS, neighbours(padded))
    ]


def apply_operator(padded, face_list):
    centre = padded[1:-1, 1:-1, 1:-1]
    result_sum = STORAGE * centre
    for face_term, beside in zip(face_list, neighbours(padded)):
        result_sum = result_sum + face_term * (centre - beside)
    return result_sum


def padded_depth(field_now):
    return jnp.pad(field_now, ((0, 0), (0, 0), (1, 1)))


def chain_solve(chain_rows):
    blocks_count = chain_rows.shape[0]
    carry_value = jnp.zeros_like(chain_rows[0, 0])
    carry_gain = jnp.zeros_like(chain_rows[0, 0])
    first_parts, first_links, last_parts, last_links = ([], [], [], [])
    for block_index in range(blocks_count):
        pivot_value = 1.0 - chain_rows[block_index, 2] * carry_gain
        first_part = (
            chain_rows[block_index, 0] - chain_rows[block_index, 2] * carry_value
        ) / pivot_value
        first_link = chain_rows[block_index, 4] / pivot_value
        carry_value = (
            chain_rows[block_index, 1]
            - chain_rows[block_index, 3] * carry_value
            + chain_rows[block_index, 3] * carry_gain * first_part
        )
        carry_gain = (
            chain_rows[block_index, 5] + chain_rows[block_index, 3] * carry_gain * first_link
        )
        first_parts.append(first_part)
        first_links.append(first_link)
        last_parts.append(carry_value)
        last_links.append(carry_gain)
    following = jnp.zeros_like(carry_value)
    last_values = [following] * blocks_count
    next_values = [following] * blocks_count
    for block_index in range(blocks_count - 1, -1, -1):
        next_values[block_index] = following
        last_values[block_index] = last_parts[block_index] - last_links[block_index] * following
        following = first_parts[block_index] - first_links[block_index] * following
    previous = [jnp.zeros_like(following)] + last_values[:-1]
    return jnp.stack(
        [
            jnp.stack([previous[block_index], next_values[block_index]])
            for block_index in range(blocks_count)
        ]
    )


def reduced_solve(chain_local):
    packed = chain_local[None]
    everyone = lax.all_gather(packed, "gx", axis=0, tiled=True)
    solved = chain_solve(everyone)
    return lax.dynamic_index_in_dim(solved, lax.axis_index("gx"), 0, keepdims=False)


def line_apply(grouped, matrices, couples):
    values = jnp.einsum("gic,cgm->igm", matrices, grouped, precision=PRECISE)
    group_count, column_count = (values.shape[1], values.shape[2])
    lower_couple = couples[0]
    upper_couple = couples[1]

    def spread(vector):
        return jnp.broadcast_to(vector[:, None], (group_count, column_count)).reshape(
            group_count * column_count
        )

    chain_local = jnp.stack(
        [
            values[0].reshape(-1),
            values[-1].reshape(-1),
            spread(lower_couple * matrices[:, 0, 0]),
            spread(lower_couple * matrices[:, -1, 0]),
            spread(upper_couple * matrices[:, 0, -1]),
            spread(upper_couple * matrices[:, -1, -1]),
        ]
    )
    solved = reduced_solve(chain_local)
    previous = solved[0].reshape(group_count, column_count)
    following = solved[1].reshape(group_count, column_count)
    first_column = jnp.transpose(matrices[:, :, 0])
    last_column = jnp.transpose(matrices[:, :, -1])
    return (
        values
        - (lower_couple[:, None] * previous)[None] * first_column[:, :, None]
        - (upper_couple[:, None] * following)[None] * last_column[:, :, None]
    )


def local(
    source_field,
    permeability,
    layer_ids,
    inverse_fine,
    couple_fine,
    inverse_coarse,
    couple_coarse,
    owner_map,
):
    block_width, planes, depth_cells = source_field.shape
    layers = inverse_fine.shape[0]
    per_layer = depth_cells // layers
    order = jnp.argsort(layer_ids, stable=True)
    restore = jnp.argsort(order, stable=True)
    halo_permeability = with_halo(permeability, (("gx", 0), ("gy", 1)), 1)
    face_list = face_terms(padded_depth(halo_permeability))

    def residual_of(field_now):
        padded = with_halo(field_now, (("gx", 0), ("gy", 1)), 1)
        return source_field - apply_operator(padded_depth(padded), face_list)

    fine_couples = couple_fine[:, :, 0]
    solution = jnp.zeros_like(source_field)
    update = source_field
    for sweep_index in range(NSWEEP):
        if sweep_index > 0:
            update = residual_of(solution)
        ordered = jnp.take(update, order, axis=2).reshape(block_width, planes, layers, per_layer)
        change = line_apply(
            jnp.transpose(ordered, (0, 2, 1, 3)).reshape(block_width, layers, planes * per_layer),
            inverse_fine,
            fine_couples,
        )
        from_shaped = jnp.transpose(
            change.reshape(block_width, layers, planes, per_layer), (0, 2, 1, 3)
        )
        solution = solution + jnp.take(
            from_shaped.reshape(block_width, planes, depth_cells), restore, axis=2
        )
    residual = residual_of(solution)
    coarse = 0.5 * (residual[:, 0::2, :] + residual[:, 1::2, :])
    coarse_sorted = jnp.take(coarse[:, 0, :], order, axis=1).reshape(block_width, layers, per_layer)
    groups = lax.axis_size("gy")
    position = lax.axis_index("gy")
    aggregates = groups // 4
    owners = owner_map[:, 0]
    own_owner = lax.dynamic_index_in_dim(owners, position, 0, keepdims=False)
    selector = (jnp.arange(aggregates, dtype=jnp.int32) == own_owner).astype(jnp.float32)
    slot_terms = selector[None, None, :, None] * coarse_sorted[:, :, None, :]
    flat_terms = slot_terms.reshape(block_width, layers * aggregates * per_layer)
    own_columns = lax.psum_scatter(flat_terms, "gy", scatter_dimension=1, tiled=True)
    own_layer = position // (groups // layers)
    matrix = lax.dynamic_index_in_dim(inverse_coarse, own_layer, 0, keepdims=True)
    couples = lax.dynamic_index_in_dim(couple_coarse[:, :, 0], own_layer, 1, keepdims=True)
    smoothed = line_apply(own_columns[:, None, :], matrix, couples)[:, 0, :]
    every_column = lax.all_gather(smoothed, "gy", axis=1, tiled=True)
    shaped = every_column.reshape(block_width, layers, aggregates, per_layer)
    picked = lax.dynamic_index_in_dim(shaped, own_owner, 2, keepdims=False)
    result = jnp.take(picked.reshape(block_width, depth_cells), restore, axis=1)
    return (solution, residual, result[:, None, :])


def solution(mesh):
    in_specs = (
        P("gx", "gy", None),
        P("gx", "gy", None),
        P(),
        P(None, "gx", None),
        P(None, None, "gx"),
        P(None, "gx", None),
        P(None, None, "gx"),
        P(),
    )
    out_specs = (P("gx", "gy", None), P("gx", "gy", None), P("gx", "gy", None))
    return jax.shard_map(local, mesh=mesh, in_specs=in_specs, out_specs=out_specs, check_vma=False)
```

profile of v0, /device:TPU:8, one launch (start us, length us, event | category | flops | bytes accessed | tf_op | source)
XLA Modules:
  0.0 583.6 jit_solution(3211472923270498532)
XLA Ops:
  7.2 3.8 sort.31
  14.5 3.2 sort.32
  24.2 4.5 convolution_bitcast_fusion.2
  29.3 13.0 %all-gather.5 = f32[8,6,512]{2,1,0:T(8,128)S(1)} all-gather(f32[1,6,512]{2,1,0:T(8,128)S(1)} %bitcast.1530), channel_id=2, replica_groups=mesh['gx'=8,'gy'=32] {'gx'}, dimensions={0}, use_global_device_ids=true | all-gather | bytes 110592 | tf_op jit(solution)/shard_map/all_gather | solution.py:97
  48.9 3.5 collective-permute-start.3
  54.4 3.9 collective-permute-start.2
  59.1 3.3 collective-permute-start.5
  64.9 4.6 collective-permute-start.4
  71.4 3.3 collective-permute-done.5
  74.8 4.9 collective-permute-done.7
  79.7 4.0 collective-permute-done.4
  83.8 4.6 collective-permute-done.6
  94.4 3.6 fusion.37
  99.3 3.0 gather_fusion.2
  104.5 4.5 convolution_bitcast_fusion.1
  109.4 22.6 %all-gather.6 = f32[8,6,512]{2,1,0:T(8,128)S(1)} all-gather(f32[1,6,512]{2,1,0:T(8,128)S(1)} %bitcast.1531), channel_id=3, replica_groups=mesh['gx'=8,'gy'=32] {'gx'}, dimensions={0}, use_global_device_ids=true | all-gather | bytes 110592 | tf_op jit(solution)/shard_map/all_gather | solution.py:97
  142.6 3.3 collective-permute-start.9
  148.0 3.4 collective-permute-start.10
  153.2 10.3 %collective-permute-done.10 = f32[514,1,256]{2,1,0:T(1,128)S(1)} collective-permute-done((f32[514,1,256]{2,1,0:T(1,128)S(1)}, f32[514,1,256]{2,1,0:T(1,128)S(1)}, u32[]{:S(2)}, u32[]{:S(2)}) %collective-permute-start.10) | collective-permute-done | bytes 526368 | tf_op jit(solution)/shard_map/ppermute | solution.py:19
  163.6 4.9 collective-permute-done.11
  170.7 4.5 fusion.20
  181.9 4.5 convolution_bitcast_fusion
  186.8 11.7 %all-gather.7 = f32[8,6,512]{2,1,0:T(8,128)S(1)} all-gather(f32[1,6,512]{2,1,0:T(8,128)S(1)} %bitcast.1529), channel_id=4, replica_groups=mesh['gx'=8,'gy'=32] {'gx'}, dimensions={0}, use_global_device_ids=true | all-gather | bytes 110592 | tf_op jit(solution)/shard_map/all_gather | solution.py:97
  201.2 3.0 gather_fusion.5
  209.3 3.3 collective-permute-start.13
  214.6 5.0 collective-permute-start.14
  223.7 7.9 %collective-permute-done.14 = f32[514,1,256]{2,1,0:T(1,128)S(1)} collective-permute-done((f32[514,1,256]{2,1,0:T(1,128)S(1)}, f32[514,1,256]{2,1,0:T(1,128)S(1)}, u32[]{:S(2)}, u32[]{:S(2)}) %collective-permute-start.14) | collective-permute-done | bytes 526368 | tf_op jit(solution)/shard_map/ppermute | solution.py:19
  231.7 6.3 %collective-permute-done.15 = f32[514,1,256]{2,1,0:T(1,128)} collective-permute-done((f32[514,1,256]{2,1,0:T(1,128)}, f32[514,1,256]{2,1,0:T(1,128)}, u32[]{:S(2)}, u32[]{:S(2)}) %collective-permute-start.15) | collective-permute-done | bytes 526368 | tf_op jit(solution)/shard_map/ppermute | solution.py:20
  241.2 3.6 fusion.3
  258.6 216.9 %reduce-scatter.2.cloned.1.call-done = f32[512,64]{0,1:T(8,128)} async-done(((f32[512,2048]{0,1:T(8,128)}), f32[512,64]{0,1:T(8,128)}) %reduce-scatter.2.cloned.1.call-update) | async-done | bytes 131088 | tf_op jit(solution)/shard_map/reduce_scatter | solution.py:186
  477.8 13.1 %all-gather.8 = f32[8,6,64]{2,1,0:T(8,128)S(1)} all-gather(f32[1,6,64]{2,1,0:T(8,128)S(1)} %bitcast.1545), channel_id=5, replica_groups=mesh['gx'=8,'gy'=32] {'gx'}, dimensions={0}, use_global_device_ids=true | all-gather | bytes 13824 | tf_op jit(solution)/shard_map/all_gather | solution.py:97
  498.7 74.4 %all-gather.11.cloned.1.call-done = f32[512,1,2048]{0,2,1:T(8,128)} async-done(((f32[512,1,64]{0,2,1:T(8,128)}), f32[512,1,2048]{0,2,1:T(8,128)}) %all-gather.11.cloned.1.call-update) | async-done | bytes 4194320 | tf_op jit(solution)/shard_map/all_gather | solution.py:191
  (255 shorter events, 94.5 us)
Async XLA Ops:
  7.2 215.1 %copy-start = (s32[32,1]{0,1:T(1,128)S(1)}, s32[32,1]{0,1:T(1,128)}, u32[]{:S(2)}) copy-start(s32[32,1]{0,1:T(1,128)} %param.19) | copy-start | bytes 388
  7.2 468.3 %reduce-scatter.2.cloned.1.call-start = ((), (), s32[]{:S(2)}) async-start(), calls=%async_computation.1 | async-start | bytes 4325376 | tf_op jit(solution)/shard_map/reduce_scatter | solution.py:186
  24.1 4.8 copy-start.19
  44.1 8.3 %copy-start.7 = (f32[512,2,256]{2,1,0:T(2,128)S(1)}, f32[512,2,256]{2,1,0:T(2,128)}, u32[]{:S(2)}) copy-start(f32[512,2,256]{2,1,0:T(2,128)} %param.13) | copy-start | bytes 3145732
  46.5 7.8 %copy-start.18 = (f32[256,512,2]{0,1,2:T(8,128)}, f32[256,512,2]{0,1,2:T(8,128)S(1)}, u32[]{:S(2)}) copy-start(f32[256,512,2]{0,1,2:T(8,128)S(1)} %copy.164) | copy-start | bytes 3145732
  46.6 11.7 %collective-permute-start.1 = (f32[1,2,256]{2,0,1:T(1,128)S(1)}, f32[1,2,256]{2,0,1:T(1,128)S(1)}, u32[]{:S(2)}, u32[]{:S(2)}) collective-permute-start(f32[1,2,256]{2,0,1:T(1,128)S(1)} %get-tuple-element.218), channel_id=1, source_target_pairs={{0,32},{32,64},{64,96},{96,128},{128,160},{160,192},{192,224},{1,3... | collective-permute-start | bytes 6152 | tf_op jit(solution)/shard_map/ppermute | solution.py:19
  48.9 9.5 %collective-permute-start.3 = (f32[1,2,256]{2,0,1:T(1,128)S(1)}, f32[1,2,256]{2,0,1:T(1,128)S(1)}, u32[]{:S(2)}, u32[]{:S(2)}) collective-permute-start(f32[1,2,256]{2,0,1:T(1,128)S(1)} %get-tuple-element.219), channel_id=1, source_target_pairs={{32,0},{64,32},{96,64},{128,96},{160,128},{192,160},{224,192},{33,... | collective-permute-start | bytes 6152 | tf_op jit(solution)/shard_map/ppermute | solution.py:20
  52.4 11.8 %collective-permute-start = (f32[1,2,256]{2,0,1:T(1,128)S(1)}, f32[1,2,256]{2,0,1:T(1,128)S(1)}, u32[]{:S(2)}, u32[]{:S(2)}) collective-permute-start(f32[1,2,256]{2,0,1:T(1,128)S(1)} %copy.165), channel_id=1, source_target_pairs={{0,32},{32,64},{64,96},{96,128},{128,160},{160,192},{192,224},{1,3... | collective-permute-start | bytes 6152 | tf_op jit(solution)/shard_map/ppermute | solution.py:19
  54.4 9.8 %collective-permute-start.2 = (f32[1,2,256]{2,0,1:T(1,128)S(1)}, f32[1,2,256]{2,0,1:T(1,128)S(1)}, u32[]{:S(2)}, u32[]{:S(2)}) collective-permute-start(f32[1,2,256]{2,0,1:T(1,128)S(1)} %copy.169), channel_id=1, source_target_pairs={{32,0},{64,32},{96,64},{128,96},{160,128},{192,160},{224,192},{33,... | collective-permute-start | bytes 6152 | tf_op jit(solution)/shard_map/ppermute | solution.py:20
  59.1 15.6 %collective-permute-start.5 = (f32[514,1,256]{2,1,0:T(1,128)S(1)}, f32[514,1,256]{2,1,0:T(1,128)S(1)}, u32[]{:S(2)}, u32[]{:S(2)}) collective-permute-start(f32[514,1,256]{2,1,0:T(1,128)S(1)} %copy.178), channel_id=1, source_target_pairs={{0,1},{1,2},{2,3},{3,4},{4,5},{5,6},{6,7},{7,8},{8,9},{9,10},{10,1... | collective-permute-start | bytes 1579016 | tf_op jit(solution)/shard_map/ppermute | solution.py:19
  62.9 16.8 %collective-permute-start.7 = (f32[514,1,256]{2,1,0:T(1,128)S(1)}, f32[514,1,256]{2,1,0:T(1,128)S(1)}, u32[]{:S(2)}, u32[]{:S(2)}) collective-permute-start(f32[514,1,256]{2,1,0:T(1,128)S(1)} %copy.183), channel_id=1, source_target_pairs={{1,0},{2,1},{3,2},{4,3},{5,4},{6,5},{7,6},{8,7},{9,8},{10,9},{11,1... | collective-permute-start | bytes 1579016 | tf_op jit(solution)/shard_map/ppermute | solution.py:20
  64.9 18.8 %collective-permute-start.4 = (f32[514,1,256]{2,1,0:T(1,128)S(1)}, f32[514,1,256]{2,1,0:T(1,128)S(1)}, u32[]{:S(2)}, u32[]{:S(2)}) collective-permute-start(f32[514,1,256]{2,1,0:T(1,128)S(1)} %copy.175), channel_id=1, source_target_pairs={{0,1},{1,2},{2,3},{3,4},{4,5},{5,6},{6,7},{7,8},{8,9},{9,10},{10,1... | collective-permute-start | bytes 1579016 | tf_op jit(solution)/shard_map/ppermute | solution.py:19
  70.1 18.4 %collective-permute-start.6 = (f32[514,1,256]{2,1,0:T(1,128)S(1)}, f32[514,1,256]{2,1,0:T(1,128)S(1)}, u32[]{:S(2)}, u32[]{:S(2)}) collective-permute-start(f32[514,1,256]{2,1,0:T(1,128)S(1)} %copy.180), channel_id=1, source_target_pairs={{1,0},{2,1},{3,2},{4,3},{5,4},{6,5},{7,6},{8,7},{9,8},{10,9},{11,1... | collective-permute-start | bytes 1579016 | tf_op jit(solution)/shard_map/ppermute | solution.py:20
  83.8 9.0 %copy-start.12 = (f32[514,1,256]{2,0,1:T(8,128)}, f32[514,1,256]{2,0,1:T(8,128)S(1)}, u32[]{:S(2)}) copy-start(f32[514,1,256]{2,0,1:T(8,128)S(1)} %copy.176) | copy-start | bytes 1579012
  140.4 5.6 collective-permute-start.8
  142.6 4.6 collective-permute-start.9
  148.0 15.6 %collective-permute-start.10 = (f32[514,1,256]{2,1,0:T(1,128)S(1)}, f32[514,1,256]{2,1,0:T(1,128)S(1)}, u32[]{:S(2)}, u32[]{:S(2)}) collective-permute-start(f32[514,1,256]{2,1,0:T(1,128)S(1)} %copy.198), channel_id=1, source_target_pairs={{0,1},{1,2},{2,3},{3,4},{4,5},{5,6},{6,7},{7,8},{8,9},{9,10},{10,1... | collective-permute-start | bytes 1579016 | tf_op jit(solution)/shard_map/ppermute | solution.py:19
  151.9 16.6 %collective-permute-start.11 = (f32[514,1,256]{2,1,0:T(1,128)S(1)}, f32[514,1,256]{2,1,0:T(1,128)S(1)}, u32[]{:S(2)}, u32[]{:S(2)}) collective-permute-start(f32[514,1,256]{2,1,0:T(1,128)S(1)} %copy.200), channel_id=1, source_target_pairs={{1,0},{2,1},{3,2},{4,3},{5,4},{6,5},{7,6},{8,7},{9,8},{10,9},{11,1... | collective-permute-start | bytes 1579016 | tf_op jit(solution)/shard_map/ppermute | solution.py:20
  163.6 7.1 %copy-start.5 = (f32[514,4,258]{2,0,1:T(8,128)S(1)}, f32[514,4,258]{2,0,1:T(8,128)}, u32[]{:S(2)}) copy-start(f32[514,4,258]{2,0,1:T(8,128)} %copy-done.4) | copy-start | bytes 6365380
  163.6 7.1 %copy-start.10 = (f32[512,2,256]{2,1,0:T(2,128)S(1)}, f32[512,2,256]{2,1,0:T(2,128)}, u32[]{:S(2)}) copy-start(f32[512,2,256]{2,1,0:T(2,128)} %param.12) | copy-start | bytes 3145732
  163.6 7.1 %copy-start.13 = (f32[514,1,256]{2,0,1:T(8,128)S(1)}, f32[514,1,256]{2,0,1:T(8,128)}, u32[]{:S(2)}) copy-start(f32[514,1,256]{2,0,1:T(8,128)} %copy-done.12) | copy-start | bytes 1579012
  163.6 7.1 %copy-start.16 = (f32[514,1,256]{2,0,1:T(8,128)S(1)}, f32[514,1,256]{2,0,1:T(8,128)}, u32[]{:S(2)}) copy-start(f32[514,1,256]{2,0,1:T(8,128)} %copy-done.15) | copy-start | bytes 1579012
  207.0 5.6 collective-permute-start.12
  209.3 4.6 collective-permute-start.13
  214.6 17.0 %collective-permute-start.14 = (f32[514,1,256]{2,1,0:T(1,128)S(1)}, f32[514,1,256]{2,1,0:T(1,128)S(1)}, u32[]{:S(2)}, u32[]{:S(2)}) collective-permute-start(f32[514,1,256]{2,1,0:T(1,128)S(1)} %copy.210), channel_id=1, source_target_pairs={{0,1},{1,2},{2,3},{3,4},{4,5},{5,6},{6,7},{7,8},{8,9},{9,10},{10,1... | collective-permute-start | bytes 1579016 | tf_op jit(solution)/shard_map/ppermute | solution.py:19
  221.0 17.0 %collective-permute-start.15 = (f32[514,1,256]{2,1,0:T(1,128)}, f32[514,1,256]{2,1,0:T(1,128)}, u32[]{:S(2)}, u32[]{:S(2)}) collective-permute-start(f32[514,1,256]{2,1,0:T(1,128)} %copy.212), channel_id=1, source_target_pairs={{1,0},{2,1},{3,2},{4,3},{5,4},{6,5},{7,6},{8,7},{9,8},{10,9},{11,1... | collective-permute-start | bytes 1579016 | tf_op jit(solution)/shard_map/ppermute | solution.py:20
  231.6 9.5 %copy-start.6 = (f32[514,4,258]{2,0,1:T(8,128)S(1)}, f32[514,4,258]{2,0,1:T(8,128)}, u32[]{:S(2)}) copy-start(f32[514,4,258]{2,0,1:T(8,128)} %copy-done.4) | copy-start | bytes 6365380
  231.7 9.5 %copy-start.8 = (f32[512,2,256]{2,1,0:T(2,128)S(1)}, f32[512,2,256]{2,1,0:T(2,128)}, u32[]{:S(2)}) copy-start(f32[512,2,256]{2,1,0:T(2,128)} %param.13) | copy-start | bytes 3145732
  231.7 9.5 %copy-start.11 = (f32[512,2,256]{2,1,0:T(2,128)S(1)}, f32[512,2,256]{2,1,0:T(2,128)}, u32[]{:S(2)}) copy-start(f32[512,2,256]{2,1,0:T(2,128)} %param.12) | copy-start | bytes 3145732
  231.7 9.5 %copy-start.14 = (f32[514,1,256]{2,0,1:T(8,128)S(1)}, f32[514,1,256]{2,0,1:T(8,128)}, u32[]{:S(2)}) copy-start(f32[514,1,256]{2,0,1:T(8,128)} %copy-done.12) | copy-start | bytes 1579012
  231.7 9.5 %copy-start.17 = (f32[514,1,256]{2,0,1:T(8,128)S(1)}, f32[514,1,256]{2,0,1:T(8,128)}, u32[]{:S(2)}) copy-start(f32[514,1,256]{2,0,1:T(8,128)} %copy-done.15) | copy-start | bytes 1579012
  248.6 324.5 %all-gather.11.cloned.1.call-start = ((), (), s32[]{:S(2)}) async-start(), calls=%async_computation.2 | async-start | bytes 4325376 | tf_op jit(solution)/shard_map/all_gather | solution.py:191
  (7 other events, 17.3 us)
Sparse Core Ops, SparseCore 0:
  248.7 226.7 reduce-scatter.1
  493.3 79.6 all-gather.10
where the time goes:
time: 593 us; the launch traced here: 584 us
  waiting for transfers between devices  340 us (57%)
  blocking collectives  60.3 us (10%)
  local copies, waits for them, and re-layouts  57.9 us (10%)
  starting transfers between devices  44.2 us (7%)
  other arithmetic  42.8 us (7%)
  between operations  22.7 us (4%)
  matrix products  15.5 us (3%)
    reduce_scatter x1, waiting for transfers between devices, local(): lax.psum_scatter(flat_terms, 'gy', scatter_dimension=1, tiled=True)  217 us
    all_gather x1, waiting for transfers between devices, local(): every_column = lax.all_gather(smoothed, 'gy', axis=1, tiled=True)  74.4 us
    all_gather x4, blocking collectives, reduced_solve(): everyone = lax.all_gather(packed, 'gx', axis=0, tiled=True)  60.3 us
    ppermute x8, waiting for transfers between devices, with_halo(): before = lax.ppermute(last, axis, up)  25.6 us
    ppermute x8, starting transfers between devices, with_halo(): before = lax.ppermute(last, axis, up)  24.9 us
    ppermute x8, waiting for transfers between devices, with_halo(): after = lax.ppermute(leading, axis, down)  23.3 us
    ppermute x8, starting transfers between devices, with_halo(): after = lax.ppermute(leading, axis, down)  19.2 us
    dot_general x4, matrix products, line_apply(): values = jnp.einsum('gic,cgm->igm', matrices, grouped, precision=PRECISE)  15.5 us
  transfers between devices with their start and end apart: 18, of which 12 were waited for; matrix products, arithmetic and copies ran while one was open for 2% of the time, Pallas kernels for 0%

commit v1 on v0

--- a/solution.py
+++ b/solution.py
@@ -7,6 +7,12 @@
 PRECISE = lax.Precision.HIGHEST
 WEIGHTS = (0.5, 0.5, 0.15, 0.15, 0.05, 0.05)
 STORAGE = 0.1
+
+
+def in_order(blocks, dim):
+    shape = list(blocks.shape[1:])
+    shape[dim] *= blocks.shape[0]
+    return jnp.moveaxis(blocks, 0, dim).reshape(shape)
 
 
 def with_halo(array, sides, width):
@@ -94,7 +100,19 @@
 
 def reduced_solve(chain_local):
     packed = chain_local[None]
-    everyone = lax.all_gather(packed, "gx", axis=0, tiled=True)
+    size = lax.axis_size("gx")
+    pairs = [(i_2, (i_2 + 1) % size) for i_2 in range(size)]
+    back = [(b, a) for a, b in pairs]
+    lower, upper = ([], [])
+    for lap in range(size - 1):
+        if lap % 2 == 0:
+            lower.append(lax.ppermute(lower[-1] if lower else packed, "gx", pairs))
+        else:
+            upper.append(lax.ppermute(upper[-1] if upper else packed, "gx", back))
+    parts = jnp.stack([*lower[::-1], packed, *upper])
+    shift = lax.axis_index("gx") - len(lower)
+    parts = parts[(jnp.arange(size) - shift) % size]
+    everyone = in_order(parts, 0)
     solved = chain_solve(everyone)
     return lax.dynamic_index_in_dim(solved, lax.axis_index("gx"), 0, keepdims=False)
 

time: 593 us -> 602 us (1.015)
  blocking collectives: 60.3 us -> 0 us
  waiting for transfers between devices: 340 us -> 372 us
  starting transfers between devices: 44.2 us -> 68.1 us
  local copies, waits for them, and re-layouts: 57.9 us -> 70 us
    all_gather x4 -> x0, blocking collectives: 60.3 us -> none  [reduced_solve(): everyone = lax.all_gather(packed, 'gx', axis=0, tiled=True)]
    ppermute x0 -> x28, waiting for transfers between devices: none -> 26.1 us  [the longest x16 24.1 us: reduced_solve(): lower.append(lax.ppermute(lower[-1] if lower else packed, 'gx', pairs))]
    ppermute x0 -> x28, starting transfers between devices: none -> 21.2 us  [the longest x12 20.9 us: reduced_solve(): upper.append(lax.ppermute(upper[-1] if upper else packed, 'gx', back))]
    reduce_scatter x1, waiting for transfers between devices: 217 us -> 224 us  [local(): lax.psum_scatter(flat_terms, 'gy', scatter_dimension=1, tiled=True)]
    unnamed x53 -> x93, local copies, waits for them, and re-layouts: 12.5 us -> 15.7 us
  transfers between devices with their start and end apart: 18 -> 46, of which waited for: 12 -> 27; matrix products, arithmetic and copies ran while one was open for 2% -> 6% of each run, Pallas kernels for 0% -> 0%
where the time goes in v1:
time: 602 us; the launch traced here: 594 us
  waiting for transfers between devices  372 us (62%)
  local copies, waits for them, and re-layouts  70 us (12%)
  starting transfers between devices  68.1 us (11%)
  other arithmetic  45.9 us (8%)
  between operations  22.8 us (4%)
  matrix products  15.5 us (3%)
    reduce_scatter x1, waiting for transfers between devices, local(): lax.psum_scatter(flat_terms, 'gy', scatter_dimension=1, tiled=True)  224 us
    all_gather x1, waiting for transfers between devices, local(): every_column = lax.all_gather(smoothed, 'gy', axis=1, tiled=True)  77.1 us
    ppermute x8, starting transfers between devices, with_halo(): before = lax.ppermute(last, axis, up)  27.7 us
    ppermute x8, waiting for transfers between devices, with_halo(): before = lax.ppermute(last, axis, up)  24.5 us
    ppermute x16, waiting for transfers between devices, reduced_solve(): lower.append(lax.ppermute(lower[-1] if lower else packed, 'gx', pairs))  24.1 us
    ppermute x12, starting transfers between devices, reduced_solve(): upper.append(lax.ppermute(upper[-1] if upper else packed, 'gx', back))  20.9 us
    ppermute x8, waiting for transfers between devices, with_halo(): after = lax.ppermute(leading, axis, down)  19.6 us
    ppermute x8, starting transfers between devices, with_halo(): after = lax.ppermute(leading, axis, down)  19.2 us
  transfers between devices with their start and end apart: 46, of which 27 were waited for; matrix products, arithmetic and copies ran while one was open for 6% of the time, Pallas kernels for 0%

profile of v1, /device:TPU:8, one launch (start us, length us, event | category | flops | bytes accessed | tf_op | source)
XLA Modules:
  0.0 593.9 jit_solution(16916186709966512093)
XLA Ops:
  7.2 3.8 sort.31
  18.5 4.5 convolution_bitcast_fusion.2
  27.4 3.6 collective-permute-start.9
  34.0 3.2 sort.32
  37.9 3.1 collective-permute-done.1
  45.5 4.2 collective-permute-start.11
  59.1 2.7 gather_fusion.5
  63.3 3.6 collective-permute-start.10
  72.6 4.7 collective-permute-start.12
  83.7 4.4 collective-permute-done.12
  88.1 4.6 collective-permute-done.14
  94.9 3.6 fusion.37
  99.9 3.0 gather_fusion.6
  105.1 4.5 convolution_bitcast_fusion.1
  110.0 3.2 collective-permute-done.15
  126.5 2.7 gather_fusion.7
  133.1 3.0 collective-permute-start.22
  145.2 10.3 %collective-permute-done.24 = f32[514,1,256]{2,1,0:T(1,128)S(1)} collective-permute-done((f32[514,1,256]{2,1,0:T(1,128)S(1)}, f32[514,1,256]{2,1,0:T(1,128)S(1)}, u32[]{:S(2)}, u32[]{:S(2)}) %collective-permute-start.24) | collective-permute-done | bytes 526368 | tf_op jit(solution)/shard_map/ppermute | solution.py:25
  155.6 6.3 %collective-permute-done.25 = f32[514,1,256]{2,1,0:T(1,128)S(1)} collective-permute-done((f32[514,1,256]{2,1,0:T(1,128)S(1)}, f32[514,1,256]{2,1,0:T(1,128)S(1)}, u32[]{:S(2)}, u32[]{:S(2)}) %collective-permute-start.25) | collective-permute-done | bytes 526368 | tf_op jit(solution)/shard_map/ppermute | solution.py:26
  164.4 4.5 fusion.20
  171.2 3.0 gather_fusion.8
  176.4 4.5 convolution_bitcast_fusion
  181.3 3.0 collective-permute-done.26
  203.3 2.8 collective-permute-start.33
  206.1 4.1 collective-permute-start.34
  212.0 6.2 %collective-permute-start.35 = (f32[514,1,256]{2,1,0:T(1,128)S(1)}, f32[514,1,256]{2,1,0:T(1,128)S(1)}, u32[]{:S(2)}, u32[]{:S(2)}) collective-permute-start(f32[514,1,256]{2,1,0:T(1,128)S(1)} %copy.210), channel_id=1, source_target_pairs={{0,1},{1,2},{2,3},{3,4},{4,5},{5,6},{6,7},{7,8},{8,9},{9,10},{10,1... | collective-permute-start | bytes 1579016 | tf_op jit(solution)/shard_map/ppermute | solution.py:25
  222.2 7.2 %collective-permute-done.35 = f32[514,1,256]{2,1,0:T(1,128)S(1)} collective-permute-done((f32[514,1,256]{2,1,0:T(1,128)S(1)}, f32[514,1,256]{2,1,0:T(1,128)S(1)}, u32[]{:S(2)}, u32[]{:S(2)}) %collective-permute-start.35) | collective-permute-done | bytes 526368 | tf_op jit(solution)/shard_map/ppermute | solution.py:25
  229.5 6.3 %collective-permute-done.36 = f32[514,1,256]{2,1,0:T(1,128)} collective-permute-done((f32[514,1,256]{2,1,0:T(1,128)}, f32[514,1,256]{2,1,0:T(1,128)}, u32[]{:S(2)}, u32[]{:S(2)}) %collective-permute-start.36) | collective-permute-done | bytes 526368 | tf_op jit(solution)/shard_map/ppermute | solution.py:26
  239.1 3.6 fusion.3
  254.6 224.2 %reduce-scatter.2.cloned.1.call-done = f32[512,64]{0,1:T(8,128)} async-done(((f32[512,2048]{0,1:T(8,128)}), f32[512,64]{0,1:T(8,128)}) %reduce-scatter.2.cloned.1.call-update) | async-done | bytes 131088 | tf_op jit(solution)/shard_map/reduce_scatter | solution.py:204
  481.1 3.0 collective-permute-done.37
  506.5 77.1 %all-gather.3.cloned.1.call-done = f32[512,1,2048]{0,2,1:T(8,128)} async-done(((f32[512,1,64]{0,2,1:T(8,128)}), f32[512,1,2048]{0,2,1:T(8,128)}) %all-gather.3.cloned.1.call-update) | async-done | bytes 4194320 | tf_op jit(solution)/shard_map/all_gather | solution.py:209
  (357 shorter events, 142.7 us)
Async XLA Ops:
  7.2 471.7 %reduce-scatter.2.cloned.1.call-start = ((), (), s32[]{:S(2)}) async-start(), calls=%async_computation.1 | async-start | bytes 4325376 | tf_op jit(solution)/shard_map/reduce_scatter | solution.py:204
  23.7 14.1 %collective-permute-start = (f32[1,6,512]{2,1,0:T(8,128)S(1)}, f32[1,6,512]{2,1,0:T(8,128)S(1)}, u32[]{:S(2)}, u32[]{:S(2)}) collective-permute-start(f32[1,6,512]{2,1,0:T(8,128)S(1)} %bitcast.1602), channel_id=1, source_target_pairs={{0,32},{32,64},{64,96},{96,128},{128,160},{160,192},{192,224},{224... | collective-permute-start | bytes 36872 | tf_op jit(solution)/shard_map/ppermute | solution.py:109
  23.7 17.4 %collective-permute-start.4 = (f32[1,6,512]{2,1,0:T(8,128)S(1)}, f32[1,6,512]{2,1,0:T(8,128)S(1)}, u32[]{:S(2)}, u32[]{:S(2)}) collective-permute-start(f32[1,6,512]{2,1,0:T(8,128)S(1)} %bitcast.1603), channel_id=1, source_target_pairs={{32,0},{64,32},{96,64},{128,96},{160,128},{192,160},{224,192},{0,2... | collective-permute-start | bytes 36872 | tf_op jit(solution)/shard_map/ppermute | solution.py:111
  25.4 15.5 %collective-permute-start.7 = (f32[1,2,256]{2,0,1:T(1,128)S(1)}, f32[1,2,256]{2,0,1:T(1,128)S(1)}, u32[]{:S(2)}, u32[]{:S(2)}) collective-permute-start(f32[1,2,256]{2,0,1:T(1,128)S(1)} %copy.165), channel_id=1, source_target_pairs={{0,32},{32,64},{64,96},{96,128},{128,160},{160,192},{192,224},{1,3... | collective-permute-start | bytes 6152 | tf_op jit(solution)/shard_map/ppermute | solution.py:25
  27.4 13.6 %collective-permute-start.9 = (f32[1,2,256]{2,0,1:T(1,128)S(1)}, f32[1,2,256]{2,0,1:T(1,128)S(1)}, u32[]{:S(2)}, u32[]{:S(2)}) collective-permute-start(f32[1,2,256]{2,0,1:T(1,128)S(1)} %copy.169), channel_id=1, source_target_pairs={{32,0},{64,32},{96,64},{128,96},{160,128},{192,160},{224,192},{33,... | collective-permute-start | bytes 6152 | tf_op jit(solution)/shard_map/ppermute | solution.py:26
  37.8 3.2 collective-permute-start.1
  41.1 11.5 %collective-permute-start.5 = (f32[1,6,512]{2,1,0:T(8,128)S(1)}, f32[1,6,512]{2,1,0:T(8,128)S(1)}, u32[]{:S(2)}, u32[]{:S(2)}) collective-permute-start(f32[1,6,512]{2,1,0:T(8,128)S(1)} %collective-permute-done.4), channel_id=1, source_target_pairs={{32,0},{64,32},{96,64},{128,96},{160,128},{192,160},{224,192},{0,2... | collective-permute-start | bytes 36872 | tf_op jit(solution)/shard_map/ppermute | solution.py:111
  44.1 9.9 %collective-permute-start.3 = (f32[1,6,512]{2,1,0:T(8,128)S(1)}, f32[1,6,512]{2,1,0:T(8,128)S(1)}, u32[]{:S(2)}, u32[]{:S(2)}) collective-permute-start(f32[1,6,512]{2,1,0:T(8,128)S(1)} %collective-permute-done.2), channel_id=1, source_target_pairs={{0,32},{32,64},{64,96},{96,128},{128,160},{160,192},{192,224},{224... | collective-permute-start | bytes 36872 | tf_op jit(solution)/shard_map/ppermute | solution.py:109
  45.5 33.6 %collective-permute-start.11 = (f32[514,1,256]{2,1,0:T(1,128)}, f32[514,1,256]{2,1,0:T(1,128)}, u32[]{:S(2)}, u32[]{:S(2)}) collective-permute-start(f32[514,1,256]{2,1,0:T(1,128)} %copy.175), channel_id=1, source_target_pairs={{0,1},{1,2},{2,3},{3,4},{4,5},{5,6},{6,7},{7,8},{8,9},{9,10},{10,1... | collective-permute-start | bytes 1579016 | tf_op jit(solution)/shard_map/ppermute | solution.py:25
  51.1 29.2 %collective-permute-start.13 = (f32[514,1,256]{2,1,0:T(1,128)}, f32[514,1,256]{2,1,0:T(1,128)}, u32[]{:S(2)}, u32[]{:S(2)}) collective-permute-start(f32[514,1,256]{2,1,0:T(1,128)} %copy.180), channel_id=1, source_target_pairs={{1,0},{2,1},{3,2},{4,3},{5,4},{6,5},{7,6},{8,7},{9,8},{10,9},{11,1... | collective-permute-start | bytes 1579016 | tf_op jit(solution)/shard_map/ppermute | solution.py:26
  63.3 5.9 collective-permute-start.10
  66.9 4.9 collective-permute-start.8
  72.6 15.5 %collective-permute-start.12 = (f32[514,1,256]{2,1,0:T(1,128)S(1)}, f32[514,1,256]{2,1,0:T(1,128)S(1)}, u32[]{:S(2)}, u32[]{:S(2)}) collective-permute-start(f32[514,1,256]{2,1,0:T(1,128)S(1)} %copy.178), channel_id=1, source_target_pairs={{0,1},{1,2},{2,3},{3,4},{4,5},{5,6},{6,7},{7,8},{8,9},{9,10},{10,1... | collective-permute-start | bytes 1579016 | tf_op jit(solution)/shard_map/ppermute | solution.py:25
  77.8 14.9 %collective-permute-start.14 = (f32[514,1,256]{2,1,0:T(1,128)S(1)}, f32[514,1,256]{2,1,0:T(1,128)S(1)}, u32[]{:S(2)}, u32[]{:S(2)}) collective-permute-start(f32[514,1,256]{2,1,0:T(1,128)S(1)} %copy.183), channel_id=1, source_target_pairs={{1,0},{2,1},{3,2},{4,3},{5,4},{6,5},{7,6},{8,7},{9,8},{10,9},{11,1... | collective-permute-start | bytes 1579016 | tf_op jit(solution)/shard_map/ppermute | solution.py:26
  109.9 3.2 collective-permute-start.15
  113.1 3.2 collective-permute-start.19
  116.3 3.5 collective-permute-start.20
  133.1 5.6 collective-permute-start.22
  136.1 3.9 collective-permute-start.23
  140.7 14.8 %collective-permute-start.24 = (f32[514,1,256]{2,1,0:T(1,128)S(1)}, f32[514,1,256]{2,1,0:T(1,128)S(1)}, u32[]{:S(2)}, u32[]{:S(2)}) collective-permute-start(f32[514,1,256]{2,1,0:T(1,128)S(1)} %copy.198), channel_id=1, source_target_pairs={{0,1},{1,2},{2,3},{3,4},{4,5},{5,6},{6,7},{7,8},{8,9},{9,10},{10,1... | collective-permute-start | bytes 1579016 | tf_op jit(solution)/shard_map/ppermute | solution.py:25
  143.9 18.0 %collective-permute-start.25 = (f32[514,1,256]{2,1,0:T(1,128)S(1)}, f32[514,1,256]{2,1,0:T(1,128)S(1)}, u32[]{:S(2)}, u32[]{:S(2)}) collective-permute-start(f32[514,1,256]{2,1,0:T(1,128)S(1)} %copy.200), channel_id=1, source_target_pairs={{1,0},{2,1},{3,2},{4,3},{5,4},{6,5},{7,6},{8,7},{9,8},{10,9},{11,1... | collective-permute-start | bytes 1579016 | tf_op jit(solution)/shard_map/ppermute | solution.py:26
  181.2 3.2 collective-permute-start.26
  184.4 3.2 collective-permute-start.30
  190.8 3.2 collective-permute-start.32
  203.3 6.9 %collective-permute-start.33 = (f32[1,2,256]{2,0,1:T(1,128)S(1)}, f32[1,2,256]{2,0,1:T(1,128)S(1)}, u32[]{:S(2)}, u32[]{:S(2)}) collective-permute-start(f32[1,2,256]{2,0,1:T(1,128)S(1)} %get-tuple-element.212), channel_id=1, source_target_pairs={{0,32},{32,64},{64,96},{96,128},{128,160},{160,192},{192,224},{1,3... | collective-permute-start | bytes 6152 | tf_op jit(solution)/shard_map/ppermute | solution.py:25
  206.1 5.2 collective-permute-start.34
  212.0 17.4 %collective-permute-start.35 = (f32[514,1,256]{2,1,0:T(1,128)S(1)}, f32[514,1,256]{2,1,0:T(1,128)S(1)}, u32[]{:S(2)}, u32[]{:S(2)}) collective-permute-start(f32[514,1,256]{2,1,0:T(1,128)S(1)} %copy.210), channel_id=1, source_target_pairs={{0,1},{1,2},{2,3},{3,4},{4,5},{5,6},{6,7},{7,8},{8,9},{9,10},{10,1... | collective-permute-start | bytes 1579016 | tf_op jit(solution)/shard_map/ppermute | solution.py:25
  219.5 16.3 %collective-permute-start.36 = (f32[514,1,256]{2,1,0:T(1,128)}, f32[514,1,256]{2,1,0:T(1,128)}, u32[]{:S(2)}, u32[]{:S(2)}) collective-permute-start(f32[514,1,256]{2,1,0:T(1,128)} %copy.212), channel_id=1, source_target_pairs={{1,0},{2,1},{3,2},{4,3},{5,4},{6,5},{7,6},{8,7},{9,8},{10,9},{11,1... | collective-permute-start | bytes 1579016 | tf_op jit(solution)/shard_map/ppermute | solution.py:26
  246.4 337.2 %all-gather.3.cloned.1.call-start = ((), (), s32[]{:S(2)}) async-start(), calls=%async_computation.2 | async-start | bytes 4325376 | tf_op jit(solution)/shard_map/all_gather | solution.py:209
  487.2 5.1 collective-permute-start.42
  490.4 3.7 collective-permute-start.40
  492.3 5.8 collective-permute-start.43
  (41 other events, 520.1 us)
Sparse Core Ops, SparseCore 0:
  246.6 232.2 reduce-scatter.1
  501.2 82.4 all-gather.2
